TPU v7x, 256 devices: a whole 4x4x8 slice. The times are simulated.
256 devices in a mesh: expert: 16 (over x, y), dp: 16 (over z, core).
Axes of the slice: x: 4, y: 4, z: 8, core: 2. Of those that a mesh axis runs over, the one named last changes fastest.
Arguments:
- tokens: bfloat16 [4096, 4096], P(('expert', 'dp')), may hold values from -6 to 6
- grad_out: bfloat16 [4096, 4096], P(('expert', 'dp')), may hold values from -6 to 6
- gate_values: bfloat16 [4096, 2], P(('expert', 'dp')), may hold values from 0.099609375 to 1
- routes: int32 [4096, 2], P(('expert', 'dp')), may hold values from 0 to 31, all different within a row; in each aligned block of 16 rows (0 to 15, 16 to 31, ...) at most 2 rows name the same one
- gate_weight: bfloat16 [32, 1536, 4096], P('expert', 'dp'), may hold values from -0.09375 to 0.09375
- up_weight: bfloat16 [32, 1536, 4096], P('expert', 'dp'), may hold values from -0.09375 to 0.09375
- down_weight: bfloat16 [32, 1536, 4096], P('expert', 'dp'), may hold values from -0.15625 to 0.15625
Outputs:
- grad_tokens: bfloat16 [4096, 4096], P(('expert', 'dp'))
- grad_gates: float32 [4096, 2], P(('expert', 'dp'))
- grad_gate_weight: bfloat16 [32, 1536, 4096], P('expert', 'dp')
- grad_up_weight: bfloat16 [32, 1536, 4096], P('expert', 'dp')
- grad_down_weight: bfloat16 [32, 1536, 4096], P('expert', 'dp')
Inputs may be any that keep to these rules, and one draw needn't show every extreme that they name: `routes`: each row names 2 different experts. In each aligned block of 16 rows (the rows of one device) no expert is named by more than 2 rows, a bound that some block reaches.
All inputs are finite; a program needn't handle non-finite values.
Results may differ from a plain program's by a relative error of at most 0.019.
Values may be sent and summed in bfloat16 or wider, within the bound.
No kernel may reach another device: no remote copies, remote signals or barrier semaphores. Data moves between devices by JAX's collectives and lax.ppermute only.
A program may use at most 128 MiB of HBM per device.

v0:
```python
import jax
import jax.numpy as jnp
from jax import lax
from jax.sharding import PartitionSpec as P

PAD = 128


def per_device(tokens, grad_out, gate_values, routes, gate_weight, up_weight, down_weight):
    f32, bf16 = (jnp.float32, jnp.bfloat16)
    tok_rows, model_width = tokens.shape
    chosen = routes.shape[1]
    local_experts = gate_weight.shape[0]
    groups = lax.axis_size("expert")
    n_dp = lax.axis_size("dp")
    experts_all = local_experts * groups
    capacity = 2 * tok_rows * chosen // experts_all
    slot_count = experts_all * capacity
    block_rows = groups * capacity
    gathered_rows = n_dp * block_rows
    width = 2 * model_width + PAD
    back_width = model_width + PAD
    flat_routes = routes.reshape(-1)
    onehot = (flat_routes[:, None] == jnp.arange(experts_all, dtype=jnp.int32)[None, :]).astype(
        jnp.int32
    )
    earlier = jnp.cumsum(onehot, axis=0) - onehot
    slot_rank = jnp.sum(earlier * onehot, axis=1)
    owner_col = flat_routes // local_experts
    local_id = flat_routes % local_experts
    slot_index = (local_id * groups + owner_col) * capacity + slot_rank
    placing = (jnp.arange(slot_count, dtype=jnp.int32)[:, None] == slot_index[None, :]).astype(f32)
    token_map = jnp.sum(placing.reshape(slot_count, tok_rows, chosen), axis=2).astype(bf16)
    slot_gates = jnp.dot(
        placing.astype(bf16), gate_values.reshape(-1), preferred_element_type=f32
    ).astype(bf16)
    x_slots = jnp.dot(token_map, tokens, preferred_element_type=f32).astype(bf16)
    dy_slots = jnp.dot(token_map, grad_out, preferred_element_type=f32).astype(bf16)
    gate_cols = jnp.concatenate(
        [slot_gates[:, None], jnp.zeros((slot_count, PAD - 1), bf16)], axis=1
    )
    payload = jnp.concatenate([x_slots, dy_slots, gate_cols], axis=1)
    payload = payload.reshape(local_experts, groups, capacity, width)
    extra_rows = (
        jnp.arange(back_width, dtype=jnp.int32)[None, :]
        == model_width + jnp.arange(2, dtype=jnp.int32)[:, None]
    ).astype(bf16)
    backs, ggw, guw, gdw = ([], [], [], [])
    for l in range(local_experts):
        with jax.named_scope(f"expert_{l}"):
            blk = lax.all_to_all(payload[l], "expert", split_axis=0, concat_axis=0, tiled=True)
            blk = blk.reshape(block_rows, width)
            rows = lax.all_gather(blk, "dp", axis=0).reshape(gathered_rows, width)
            inputs = rows[:, :model_width]
            upstream = rows[:, model_width : 2 * model_width]
            weighting = rows[:, 2 * model_width].astype(f32)[:, None]
            gw, uw, dw = (gate_weight[l], up_weight[l], down_weight[l])
            gate_pre = jnp.einsum("rd,hd->rh", inputs, gw, preferred_element_type=f32)
            up_pre = jnp.einsum("rd,hd->rh", inputs, uw, preferred_element_type=f32)
            back_hidden = jnp.einsum("rd,hd->rh", upstream, dw, preferred_element_type=f32)
            sigmoid_gate = jax.nn.sigmoid(gate_pre)
            activated = gate_pre * sigmoid_gate
            hidden = activated * up_pre
            gate_part = jnp.sum(back_hidden * hidden, axis=1)
            scaled = weighting * back_hidden
            grad_gate_pre = (
                scaled * up_pre * sigmoid_gate * (1.0 + gate_pre * (1.0 - sigmoid_gate))
            ).astype(bf16)
            grad_up_pre = (scaled * activated).astype(bf16)
            weighted_hidden = (weighting * hidden).astype(bf16)
            hi = gate_part.astype(bf16)
            lo = (gate_part - hi.astype(f32)).astype(bf16)
            lhs = jnp.concatenate([grad_gate_pre, grad_up_pre, hi[:, None], lo[:, None]], axis=1)
            stacked = jnp.pad(jnp.concatenate([gw, uw], axis=0), ((0, 0), (0, PAD)))
            rhs = jnp.concatenate([stacked, extra_rows], axis=0)
            back = jnp.dot(lhs, rhs, preferred_element_type=f32).astype(bf16)
            backs.append(back.reshape(n_dp, block_rows, back_width))
            ggw.append(
                jnp.einsum("rh,rd->hd", grad_gate_pre, inputs, preferred_element_type=f32).astype(
                    bf16
                )
            )
            guw.append(
                jnp.einsum("rh,rd->hd", grad_up_pre, inputs, preferred_element_type=f32).astype(
                    bf16
                )
            )
            gdw.append(
                jnp.einsum(
                    "rh,rd->hd", weighted_hidden, upstream, preferred_element_type=f32
                ).astype(bf16)
            )
    back = lax.psum_scatter(jnp.concatenate(backs, axis=1), "dp", scatter_dimension=0, tiled=True)
    back = back.reshape(local_experts, groups, capacity, back_width)
    returned = lax.all_to_all(back, "expert", split_axis=1, concat_axis=1, tiled=True)
    returned = returned.reshape(slot_count, back_width)
    grad_tokens = lax.dot_general(
        token_map, returned[:, :model_width], (((0,), (0,)), ((), ())), preferred_element_type=f32
    ).astype(bf16)
    gate_back = returned[:, model_width].astype(f32) + returned[:, model_width + 1].astype(f32)
    grad_gates = jnp.dot(gate_back, placing, precision=lax.Precision.HIGHEST).reshape(
        tok_rows, chosen
    )
    return (grad_tokens, grad_gates, jnp.stack(ggw), jnp.stack(guw), jnp.stack(gdw))


def solution(mesh):
    rows = P(("expert", "dp"), None)
    blocks = P("expert", "dp", None)
    return jax.shard_map(
        per_device,
        mesh=mesh,
        in_specs=(rows, rows, rows, rows, blocks, blocks, blocks),
        out_specs=(rows, rows, blocks, blocks, blocks),
        check_vma=False,
    )
```

profile of v0, /device:TPU:8, one launch (start us, length us, event | category | flops | bytes accessed | tf_op | source)
XLA Modules:
  0.0 272.8 jit_solution(8301096907189134309)
XLA Ops:
  7.2 0.0 all-gather.3.cloned.1.call-start
  7.2 0.8 copy.53
  8.0 0.1 eq.72
  8.1 0.1 fusion.60
  8.2 0.1 reduce_window_sum.11
  8.2 0.2 select_reduce_fusion
  8.4 0.1 reduce_sum.43
  8.5 0.8 copy.59
  9.3 0.1 reshape.191
  9.4 0.1 fusion.33
  9.5 0.1 copy.60
  9.7 0.1 copy.58
  9.7 0.1 convert_reduce_fusion.2
  9.8 0.3 convolution_convert_fusion.8
  10.1 1.2 convolution_convert_fusion.9
  11.4 0.8 concatenate.24
  12.2 0.1 fusion.81
  12.2 0.2 squeeze.28
  12.5 17.7 %all_to_all.15 = bf16[16,2,8320]{2,1,0:T(2,128)(2,1)S(1)} all-to-all(bf16[16,2,8320]{2,1,0:T(2,128)(2,1)S(1)} %squeeze.28), channel_id=1, replica_groups=mesh['expert'=16,'dp'=16] {'expert'}, dimensions={0} | all-to-all | bytes 1064960 | tf_op jit(solution)/shard_map/expert_0/all_to_all | solution.py:51
  30.1 1.0 reshape.181
  31.1 0.0 all-gather.3.cloned.1.call-update
  31.1 0.0 all-gather.5.cloned.1.call-start
  31.2 0.2 squeeze.32
  31.4 14.0 %all_to_all.16 = bf16[16,2,8320]{2,1,0:T(2,128)(2,1)S(1)} all-to-all(bf16[16,2,8320]{2,1,0:T(2,128)(2,1)S(1)} %squeeze.32), channel_id=1, replica_groups=mesh['expert'=16,'dp'=16] {'expert'}, dimensions={0} | all-to-all | bytes 1064960 | tf_op jit(solution)/shard_map/expert_1/all_to_all | solution.py:51
  45.4 1.0 reshape.184
  46.4 0.2 reduce-scatter.2.cloned.1.call-start
  46.6 1.5 slice_bitcast_fusion.2
  48.1 0.1 slice_bitcast_fusion.3
  48.2 0.2 fusion.30
  48.5 0.1 compare_convert_fusion
  48.6 39.4 %all-gather.3.cloned.1.call-done = bf16[16,32,8320]{2,1,0:T(8,128)(2,1)} async-done(((bf16[1,32,8320]{2,1,0:T(8,128)(2,1)}), bf16[16,32,8320]{2,1,0:T(8,128)(2,1)}) %all-gather.3.cloned.1.call-update) | async-done | bytes 8519696 | tf_op jit(solution)/shard_map/expert_0/all_gather | solution.py:53
  87.9 1.0 convert_reduce_fusion.1
  89.0 4.5 %fusion.26 = f32[512,96]{0,1:T(8,128)} fusion(bf16[512,8320]{1,0:T(8,128)(2,1)} %bitcast.78, bf16[2,96,4096]{2,1,0:T(8,128)(2,1)} %param.12), kind=kOutput, calls=%fused_computation.39 | convolution fusion | flops 402653184 | bytes 5177344 | tf_op jit(solution)/shard_map/expert_0/rd,hd->rh/dot_general | solution.py:59
  93.5 51.9 %all-gather.5.cloned.1.call-done = bf16[16,32,8320]{2,1,0:T(8,128)(2,1)} async-done(((bf16[1,32,8320]{2,1,0:T(8,128)(2,1)}), bf16[16,32,8320]{2,1,0:T(8,128)(2,1)}) %all-gather.5.cloned.1.call-update) | async-done | bytes 8519696 | tf_op jit(solution)/shard_map/expert_1/all_gather | solution.py:53
  145.4 4.0 %fusion.20 = f32[512,96]{0,1:T(8,128)S(1)} fusion(bf16[512,8320]{1,0:T(8,128)(2,1)} %bitcast.70, bf16[2,96,4096]{2,1,0:T(8,128)(2,1)} %param.12), kind=kOutput, calls=%fused_computation.33 | convolution fusion | flops 402653184 | bytes 5177344 | tf_op jit(solution)/shard_map/expert_1/rd,hd->rh/dot_general | solution.py:59
  149.4 1.5 convert_reduce_fusion
  150.9 4.0 %fusion.10 = f32[512,96]{0,1:T(8,128)S(1)} fusion(bf16[512,8320]{1,0:T(8,128)(2,1)} %bitcast.79, bf16[2,96,4096]{2,1,0:T(8,128)(2,1)} %param.13), kind=kOutput, calls=%fused_computation.22 | convolution fusion | flops 402653184 | bytes 5177344 | tf_op jit(solution)/shard_map/expert_0/rd,hd->rh/dot_general | solution.py:60
  154.9 1.4 fusion.7
  156.3 0.2 copy-done.2
  156.5 2.1 multiply_convert_fusion.5
  158.6 2.1 multiply_convert_fusion.3
  160.7 3.4 %convolution_convert_fusion.1 = bf16[512,4224]{1,0:T(8,128)(2,1)} fusion(bf16[2,4224]{1,0:T(2,128)(2,1)S(1)} %compare_convert_fusion, bf16[192,4224]{1,0:T(8,128)(2,1)S(1)} %get-tuple-element.19, bf16[512,1]{0,1:T(2,128)(2,1)S(1)} %subtract_convert_fusion.1, bf16[512,1]{0,1:T(2,128)(2,1)S(1)} %convert_element_type.167, ...), kind=kOutput, calls=%fused_computation.2 | convolution fusion | flops 845358080 | bytes 6162944 | tf_op jit(solution)/shard_map/expert_0/dot_general | solution.py:76
  164.1 3.5 %convolution_convert_fusion = bf16[512,4224]{1,0:T(8,128)(2,1)} fusion(bf16[2,4224]{1,0:T(2,128)(2,1)S(1)} %compare_convert_fusion, bf16[192,4224]{1,0:T(8,128)(2,1)S(1)} %get-tuple-element.20, bf16[512,1]{0,1:T(2,128)(2,1)S(1)} %subtract_convert_fusion, bf16[512,1]{0,1:T(2,128)(2,1)S(1)} %convert_element_type.174, ...), kind=kOutput, calls=%fused_computation.1 | convolution fusion | flops 845358080 | bytes 6162944 | tf_op jit(solution)/shard_map/expert_1/dot_general | solution.py:76
  167.6 7.8 %pad_maximum_fusion = bf16[16,64,4224]{2,1,0:T(8,128)(2,1)} fusion(bf16[16,32,4224]{2,1,0:T(8,128)(2,1)} %bitcast.65, bf16[16,32,4224]{2,1,0:T(8,128)(2,1)} %bitcast.64), kind=kLoop, calls=%fused_computation | loop fusion | flops 17301504 | bytes 17301504 | tf_op jit(solution)/shard_map/concatenate | solution.py:93
  175.4 0.1 iota_compare_fusion.2
  175.5 0.8 copy-done.7
  176.3 3.0 %fusion = bf16[1,96,4096]{2,1,0:T(8,128)(2,1)S(1)} fusion(bf16[512,96]{0,1:T(8,128)(2,1)S(1)} %copy-done.7, bf16[512,8320]{1,0:T(8,128)(2,1)} %bitcast.80), kind=kOutput, calls=%fused_computation.9 | convolution fusion | flops 403046400 | bytes 5079040 | tf_op jit(solution)/shard_map/expert_0/rh,rd->hd/dot_general | solution.py:79
  179.3 3.0 %fusion.2 = bf16[1,96,4096]{2,1,0:T(8,128)(2,1)S(1)} fusion(bf16[512,96]{0,1:T(8,128)(2,1)S(1)} %get-tuple-element.15, bf16[512,8320]{1,0:T(8,128)(2,1)} %bitcast.81), kind=kOutput, calls=%fused_computation.11 | convolution fusion | flops 403046400 | bytes 5079040 | tf_op jit(solution)/shard_map/expert_0/rh,rd->hd/dot_general | solution.py:84
  182.4 3.0 %fusion.1 = bf16[1,96,4096]{2,1,0:T(8,128)(2,1)S(1)} fusion(bf16[512,96]{0,1:T(8,128)(2,1)S(1)} %copy-done.11, bf16[512,8320]{1,0:T(8,128)(2,1)} %bitcast.72), kind=kOutput, calls=%fused_computation.10 | convolution fusion | flops 403046400 | bytes 5079040 | tf_op jit(solution)/shard_map/expert_1/rh,rd->hd/dot_general | solution.py:79
  185.4 3.1 %fusion.3 = bf16[1,96,4096]{2,1,0:T(8,128)(2,1)S(1)} fusion(bf16[512,96]{0,1:T(8,128)(2,1)S(1)} %copy-done.9, bf16[512,8320]{1,0:T(8,128)(2,1)} %bitcast.73), kind=kOutput, calls=%fused_computation.12 | convolution fusion | flops 403046400 | bytes 5079040 | tf_op jit(solution)/shard_map/expert_1/rh,rd->hd/dot_general | solution.py:84
  188.5 3.2 %fusion.4 = bf16[1,96,4096]{2,1,0:T(8,128)(2,1)S(1)} fusion(bf16[512,8320]{1,0:T(8,128)(2,1)} %bitcast.82, f32[512]{0:T(512)S(1)} %convert_reduce_fusion.1, f32[512,96]{0,1:T(8,128)S(1)} %copy-done.16, f32[512,96]{0,1:T(8,128)S(1)} %copy-done.17), kind=kOutput, calls=%fused_computation.13 | convolution fusion | flops 403390464 | bytes 5376000 | tf_op jit(solution)/shard_map/expert_0/rh,rd->hd/dot_general | solution.py:89
  191.8 1.9 pad_maximum_fusion.5
  193.7 51.7 %reduce-scatter.2.cloned.1.call-done = bf16[1,64,4224]{2,1,0:T(8,128)(2,1)} async-done(((bf16[16,64,4224]{2,1,0:T(8,128)(2,1)}), bf16[1,64,4224]{2,1,0:T(8,128)(2,1)}) %reduce-scatter.2.cloned.1.call-update) | async-done | bytes 540688 | tf_op jit(solution)/shard_map/reduce_scatter | solution.py:93
  245.4 1.2 reshape.187
  246.6 1.2 copy.61
  247.8 7.3 %all-to-all-start.2 = ((bf16[2,16,2,4224]{3,2,0,1:T(2,128)(2,1)}), bf16[2,16,2,4224]{3,2,0,1:T(2,128)(2,1)S(1)}, u32[]{:S(2)}, u32[]{:S(2)}) async-start(bf16[2,16,2,4224]{3,2,0,1:T(2,128)(2,1)} %copy.61), calls=%async_computation.3 | async-start | bytes 1081344 | tf_op jit(solution)/shard_map/all_to_all | solution.py:95
  255.1 3.0 %fusion.5 = bf16[1,96,4096]{2,1,0:T(8,128)(2,1)S(1)} fusion(bf16[512,8320]{1,0:T(8,128)(2,1)} %bitcast.74, f32[512]{0:T(512)S(1)} %convert_reduce_fusion, f32[512,96]{0,1:T(8,128)S(1)} %copy-done.13, f32[512,96]{0,1:T(8,128)S(1)} %copy-done.14), kind=kOutput, calls=%fused_computation.14 | convolution fusion | flops 403390464 | bytes 5376000 | tf_op jit(solution)/shard_map/expert_1/rh,rd->hd/dot_general | solution.py:89
  258.1 1.3 pad_maximum_fusion.7
  259.4 4.5 %all-to-all-done.2 = bf16[2,16,2,4224]{3,2,0,1:T(2,128)(2,1)S(1)} async-done(((bf16[2,16,2,4224]{3,2,0,1:T(2,128)(2,1)}), bf16[2,16,2,4224]{3,2,0,1:T(2,128)(2,1)S(1)}, u32[]{:S(2)}, u32[]{:S(2)}) %all-to-all-start.2) | async-done | bytes 540704 | tf_op jit(solution)/shard_map/all_to_all | solution.py:95
  263.9 0.4 copy.62
  264.3 0.2 reshape.188
  264.5 0.8 convolution_convert_fusion.10
  265.3 0.2 add_reduce_fusion
  265.5 0.8 fusion.61
  (45 shorter events, 0.2 us)
Async XLA Ops:
  7.2 2.6 copy-start
  7.2 80.8 %all-gather.3.cloned.1.call-start = ((), (), s32[]{:S(2)}) async-start(), calls=%async_computation.4 | async-start | bytes 9052160 | tf_op jit(solution)/shard_map/expert_0/all_gather | solution.py:53
  31.1 114.3 %all-gather.5.cloned.1.call-start = ((), (), s32[]{:S(2)}) async-start(), calls=%async_computation.5 | async-start | bytes 9052160 | tf_op jit(solution)/shard_map/expert_1/all_gather | solution.py:53
  31.2 16.9 %copy-start.1 = (bf16[2,96,4096]{2,1,0:T(8,128)(2,1)S(1)}, bf16[2,96,4096]{2,1,0:T(8,128)(2,1)}, u32[]{:S(2)}) copy-start(bf16[2,96,4096]{2,1,0:T(8,128)(2,1)} %param.12) | copy-start | bytes 4718596
  46.4 199.0 %reduce-scatter.2.cloned.1.call-start = ((), (), s32[]{:S(2)}) async-start(), calls=%async_computation.6 | async-start | bytes 9191424 | tf_op jit(solution)/shard_map/reduce_scatter | solution.py:93
  145.4 9.4 %copy-start.3 = (bf16[16,32,8320]{2,1,0:T(8,128)(2,1)S(1)}, bf16[16,32,8320]{2,1,0:T(8,128)(2,1)}, u32[]{:S(2)}) copy-start(bf16[16,32,8320]{2,1,0:T(8,128)(2,1)} %all-gather.5.cloned.1.call-done) | copy-start | bytes 25559044
  145.4 9.5 %copy-start.5 = (bf16[2,96,4096]{2,1,0:T(8,128)(2,1)S(1)}, bf16[2,96,4096]{2,1,0:T(8,128)(2,1)}, u32[]{:S(2)}) copy-start(bf16[2,96,4096]{2,1,0:T(8,128)(2,1)} %param.13) | copy-start | bytes 4718596
  149.4 9.2 %copy-start.12 = (f32[512,96]{0,1:T(8,128)}, f32[512,96]{0,1:T(8,128)S(1)}, u32[]{:S(2)}) copy-start(f32[512,96]{0,1:T(8,128)S(1)} %fusion.20) | copy-start | bytes 589828
  150.8 5.4 %copy-start.4 = (bf16[16,32,8320]{2,1,0:T(8,128)(2,1)S(1)}, bf16[16,32,8320]{2,1,0:T(8,128)(2,1)}, u32[]{:S(2)}) copy-start(bf16[16,32,8320]{2,1,0:T(8,128)(2,1)} %all-gather.3.cloned.1.call-done) | copy-start | bytes 25559044
  154.8 1.6 copy-start.2
  154.9 1.6 copy-start.15
  158.6 2.1 copy-start.6
  160.7 6.9 %copy-start.8 = (bf16[512,96]{0,1:T(8,128)(2,1)}, bf16[512,96]{0,1:T(8,128)(2,1)S(1)}, u32[]{:S(2)}) copy-start(bf16[512,96]{0,1:T(8,128)(2,1)S(1)} %get-tuple-element.16) | copy-start | bytes 294916
  160.7 6.9 %copy-start.10 = (bf16[512,96]{0,1:T(8,128)(2,1)}, bf16[512,96]{0,1:T(8,128)(2,1)S(1)}, u32[]{:S(2)}) copy-start(bf16[512,96]{0,1:T(8,128)(2,1)S(1)} %get-tuple-element.13) | copy-start | bytes 294916
  175.4 0.9 copy-start.7
  179.3 3.1 %copy-start.11 = (bf16[512,96]{0,1:T(8,128)(2,1)S(1)}, bf16[512,96]{0,1:T(8,128)(2,1)}, u32[]{:S(2)}) copy-start(bf16[512,96]{0,1:T(8,128)(2,1)} %copy-done.10) | copy-start | bytes 294916
  182.3 3.0 %copy-start.9 = (bf16[512,96]{0,1:T(8,128)(2,1)S(1)}, bf16[512,96]{0,1:T(8,128)(2,1)}, u32[]{:S(2)}) copy-start(bf16[512,96]{0,1:T(8,128)(2,1)} %copy-done.8) | copy-start | bytes 294916
  185.4 3.1 %copy-start.16 = (f32[512,96]{0,1:T(8,128)S(1)}, f32[512,96]{0,1:T(8,128)}, u32[]{:S(2)}) copy-start(f32[512,96]{0,1:T(8,128)} %fusion.26) | copy-start | bytes 589828
  185.4 3.1 %copy-start.17 = (f32[512,96]{0,1:T(8,128)S(1)}, f32[512,96]{0,1:T(8,128)}, u32[]{:S(2)}) copy-start(f32[512,96]{0,1:T(8,128)} %get-tuple-element.18) | copy-start | bytes 589828
  191.7 63.3 %copy-start.13 = (f32[512,96]{0,1:T(8,128)S(1)}, f32[512,96]{0,1:T(8,128)}, u32[]{:S(2)}) copy-start(f32[512,96]{0,1:T(8,128)} %copy-done.12) | copy-start | bytes 589828
  191.7 63.3 %copy-start.14 = (f32[512,96]{0,1:T(8,128)S(1)}, f32[512,96]{0,1:T(8,128)}, u32[]{:S(2)}) copy-start(f32[512,96]{0,1:T(8,128)} %get-tuple-element.17) | copy-start | bytes 589828
  247.8 16.1 %all-to-all-start.2 = ((bf16[2,16,2,4224]{3,2,0,1:T(2,128)(2,1)}), bf16[2,16,2,4224]{3,2,0,1:T(2,128)(2,1)S(1)}, u32[]{:S(2)}, u32[]{:S(2)}) async-start(bf16[2,16,2,4224]{3,2,0,1:T(2,128)(2,1)} %copy.61), calls=%async_computation.3 | async-start | bytes 1081344 | tf_op jit(solution)/shard_map/all_to_all | solution.py:95
Sparse Core Ops, SparseCore 0:
  31.3 56.6 all-gather.2
  90.3 55.0 all-gather.4
  175.5 69.8 reduce-scatter.1
where the time goes:
time: 273 us
  waiting for transfers between devices  148 us (54%)
  matrix products  46.5 us (17%)
  blocking collectives  31.6 us (12%)
  other arithmetic  14.5 us (5%)
  between operations  14.1 us (5%)
  local copies, waits for them, and re-layouts  10.9 us (4%)
  starting transfers between devices  7.56 us (3%)
    all_gather x2, waiting for transfers between devices, per_device(): rows = lax.all_gather(blk, 'dp', axis=0).reshape(gathered_rows, width)  91.3 us
    reduce_scatter x1, waiting for transfers between devices, per_device(): lax.psum_scatter(jnp.concatenate(backs, axis=1), 'dp', scatter_dimension=...  51.7 us
    all_to_all x2, blocking collectives, per_device(): lax.all_to_all(payload[l], 'expert', split_axis=0, concat_axis=0, tiled=T...  31.6 us
    dot_general x2, matrix products, per_device(): up_pre = jnp.einsum('rd,hd->rh', inputs, uw, preferred_element_type=f32)  8.46 us
    concatenate x1, other arithmetic, per_device(): jnp.concatenate(backs, axis=1)  7.8 us
    all_to_all x1, starting transfers between devices, per_device(): lax.all_to_all(back, 'expert', split_axis=1, concat_axis=1, tiled=True)  7.26 us
    dot_general x2, matrix products, per_device(): back = jnp.dot(lhs, rhs, preferred_element_type=f32).astype(bf16)  6.85 us
    dot_general x2, matrix products, per_device(): jnp.einsum('rh,rd->hd', weighted_hidden, upstream, preferred_element_type...  6.2 us
  transfers between devices with their start and end apart: 4, of which 4 were waited for; matrix products, arithmetic and copies ran while one was open for 11% of the time, Pallas kernels for 0%

commit v1 on v0

--- a/solution.py
+++ b/solution.py
@@ -92,7 +92,10 @@
             )
     back = lax.psum_scatter(jnp.concatenate(backs, axis=1), "dp", scatter_dimension=0, tiled=True)
     back = back.reshape(local_experts, groups, capacity, back_width)
-    returned = lax.all_to_all(back, "expert", split_axis=1, concat_axis=1, tiled=True)
+    returned = jnp.concatenate(
+        lax.all_to_all(jnp.stack(jnp.split(back, lax.axis_size("expert"), axis=1)), "expert", 0, 0),
+        axis=1,
+    )
     returned = returned.reshape(slot_count, back_width)
     grad_tokens = lax.dot_general(
         token_map, returned[:, :model_width], (((0,), (0,)), ((), ())), preferred_element_type=f32

time: 273 us -> 282 us (1.033)
  local copies, waits for them, and re-layouts: 10.9 us -> 19.9 us
    unnamed x38 -> x53, local copies, waits for them, and re-layouts: 2.62 us -> 12.1 us
where the time goes in v1:
time: 282 us
  waiting for transfers between devices  148 us (52%)
  matrix products  46.4 us (16%)
  blocking collectives  31.6 us (11%)
  local copies, waits for them, and re-layouts  19.9 us (7%)
  other arithmetic  14.5 us (5%)
  between operations  14.2 us (5%)
  starting transfers between devices  7.56 us (3%)
    all_gather x2, waiting for transfers between devices, per_device(): rows = lax.all_gather(blk, 'dp', axis=0).reshape(gathered_rows, width)  91.3 us
    reduce_scatter x1, waiting for transfers between devices, per_device(): lax.psum_scatter(jnp.concatenate(backs, axis=1), 'dp', scatter_dimension=...  51.7 us
    all_to_all x2, blocking collectives, per_device(): lax.all_to_all(payload[l], 'expert', split_axis=0, concat_axis=0, tiled=T...  31.6 us
    unnamed x53, local copies, waits for them, and re-layouts  12.1 us
    dot_general x2, matrix products, per_device(): up_pre = jnp.einsum('rd,hd->rh', inputs, uw, preferred_element_type=f32)  8.46 us
    concatenate x1, other arithmetic, per_device(): jnp.concatenate(backs, axis=1)  7.8 us
    all_to_all x1, starting transfers between devices, per_device(): lax.all_to_all(jnp.stack(jnp.split(back, lax.axis_size('expert'), axis=1)...  7.26 us
    dot_general x2, matrix products, per_device(): back = jnp.dot(lhs, rhs, preferred_element_type=f32).astype(bf16)  6.85 us
  transfers between devices with their start and end apart: 4, of which 4 were waited for; matrix products, arithmetic and copies ran while one was open for 11% of the time, Pallas kernels for 0%

profile of v1, /device:TPU:8, one launch (start us, length us, event | category | flops | bytes accessed | tf_op | source)
XLA Modules:
  0.0 281.8 jit_solution(5443694744459264933)
XLA Ops:
  7.2 0.8 copy.61
  8.2 0.2 select_reduce_fusion
  8.5 0.8 copy.67
  9.4 0.1 fusion.33
  9.8 0.3 convolution_convert_fusion.8
  10.1 1.2 convolution_convert_fusion.9
  11.4 0.8 concatenate.24
  12.2 0.2 squeeze.28
  12.5 17.7 %all_to_all.15 = bf16[16,2,8320]{2,1,0:T(2,128)(2,1)S(1)} all-to-all(bf16[16,2,8320]{2,1,0:T(2,128)(2,1)S(1)} %squeeze.28), channel_id=1, replica_groups=mesh['expert'=16,'dp'=16] {'expert'}, dimensions={0} | all-to-all | bytes 1064960 | tf_op jit(solution)/shard_map/expert_0/all_to_all | solution.py:51
  30.1 1.0 reshape.181
  31.2 0.2 squeeze.32
  31.4 14.0 %all_to_all.16 = bf16[16,2,8320]{2,1,0:T(2,128)(2,1)S(1)} all-to-all(bf16[16,2,8320]{2,1,0:T(2,128)(2,1)S(1)} %squeeze.32), channel_id=1, replica_groups=mesh['expert'=16,'dp'=16] {'expert'}, dimensions={0} | all-to-all | bytes 1064960 | tf_op jit(solution)/shard_map/expert_1/all_to_all | solution.py:51
  45.4 1.0 reshape.184
  46.4 0.2 reduce-scatter.2.cloned.1.call-start
  46.6 1.5 slice_bitcast_fusion.2
  48.2 0.2 fusion.30
  48.6 39.4 %all-gather.3.cloned.1.call-done = bf16[16,32,8320]{2,1,0:T(8,128)(2,1)} async-done(((bf16[1,32,8320]{2,1,0:T(8,128)(2,1)}), bf16[16,32,8320]{2,1,0:T(8,128)(2,1)}) %all-gather.3.cloned.1.call-update) | async-done | bytes 8519696 | tf_op jit(solution)/shard_map/expert_0/all_gather | solution.py:53
  87.9 1.0 convert_reduce_fusion.1
  89.0 4.5 %fusion.26 = f32[512,96]{0,1:T(8,128)} fusion(bf16[512,8320]{1,0:T(8,128)(2,1)} %bitcast.146, bf16[2,96,4096]{2,1,0:T(8,128)(2,1)} %param.12), kind=kOutput, calls=%fused_computation.39 | convolution fusion | flops 402653184 | bytes 5177344 | tf_op jit(solution)/shard_map/expert_0/rd,hd->rh/dot_general | solution.py:59
  93.5 51.9 %all-gather.5.cloned.1.call-done = bf16[16,32,8320]{2,1,0:T(8,128)(2,1)} async-done(((bf16[1,32,8320]{2,1,0:T(8,128)(2,1)}), bf16[16,32,8320]{2,1,0:T(8,128)(2,1)}) %all-gather.5.cloned.1.call-update) | async-done | bytes 8519696 | tf_op jit(solution)/shard_map/expert_1/all_gather | solution.py:53
  145.4 4.0 %fusion.20 = f32[512,96]{0,1:T(8,128)S(1)} fusion(bf16[512,8320]{1,0:T(8,128)(2,1)} %bitcast.138, bf16[2,96,4096]{2,1,0:T(8,128)(2,1)} %param.12), kind=kOutput, calls=%fused_computation.33 | convolution fusion | flops 402653184 | bytes 5177344 | tf_op jit(solution)/shard_map/expert_1/rd,hd->rh/dot_general | solution.py:59
  149.4 1.5 convert_reduce_fusion
  150.9 4.0 %fusion.10 = f32[512,96]{0,1:T(8,128)S(1)} fusion(bf16[512,8320]{1,0:T(8,128)(2,1)} %bitcast.147, bf16[2,96,4096]{2,1,0:T(8,128)(2,1)} %param.13), kind=kOutput, calls=%fused_computation.22 | convolution fusion | flops 402653184 | bytes 5177344 | tf_op jit(solution)/shard_map/expert_0/rd,hd->rh/dot_general | solution.py:60
  154.9 1.4 fusion.7
  156.3 0.2 copy-done.2
  156.5 2.1 multiply_convert_fusion.5
  158.6 2.1 multiply_convert_fusion.3
  160.7 3.4 %convolution_convert_fusion.1 = bf16[512,4224]{1,0:T(8,128)(2,1)} fusion(bf16[2,4224]{1,0:T(2,128)(2,1)S(1)} %compare_convert_fusion, bf16[192,4224]{1,0:T(8,128)(2,1)S(1)} %get-tuple-element.19, bf16[512,1]{0,1:T(2,128)(2,1)S(1)} %subtract_convert_fusion.1, bf16[512,1]{0,1:T(2,128)(2,1)S(1)} %convert_element_type.167, ...), kind=kOutput, calls=%fused_computation.2 | convolution fusion | flops 845358080 | bytes 6162944 | tf_op jit(solution)/shard_map/expert_0/dot_general | solution.py:76
  164.1 3.5 %convolution_convert_fusion = bf16[512,4224]{1,0:T(8,128)(2,1)} fusion(bf16[2,4224]{1,0:T(2,128)(2,1)S(1)} %compare_convert_fusion, bf16[192,4224]{1,0:T(8,128)(2,1)S(1)} %get-tuple-element.20, bf16[512,1]{0,1:T(2,128)(2,1)S(1)} %subtract_convert_fusion, bf16[512,1]{0,1:T(2,128)(2,1)S(1)} %convert_element_type.174, ...), kind=kOutput, calls=%fused_computation.1 | convolution fusion | flops 845358080 | bytes 6162944 | tf_op jit(solution)/shard_map/expert_1/dot_general | solution.py:76
  167.6 7.8 %pad_maximum_fusion = bf16[16,64,4224]{2,1,0:T(8,128)(2,1)} fusion(bf16[16,32,4224]{2,1,0:T(8,128)(2,1)} %bitcast.132, bf16[16,32,4224]{2,1,0:T(8,128)(2,1)} %bitcast.131), kind=kLoop, calls=%fused_computation | loop fusion | flops 17301504 | bytes 17301504 | tf_op jit(solution)/shard_map/concatenate | solution.py:93
  175.5 0.8 copy-done.7
  176.3 3.0 %fusion = bf16[1,96,4096]{2,1,0:T(8,128)(2,1)S(1)} fusion(bf16[512,96]{0,1:T(8,128)(2,1)S(1)} %copy-done.7, bf16[512,8320]{1,0:T(8,128)(2,1)} %bitcast.148), kind=kOutput, calls=%fused_computation.9 | convolution fusion | flops 403046400 | bytes 5079040 | tf_op jit(solution)/shard_map/expert_0/rh,rd->hd/dot_general | solution.py:79
  179.3 3.0 %fusion.2 = bf16[1,96,4096]{2,1,0:T(8,128)(2,1)S(1)} fusion(bf16[512,96]{0,1:T(8,128)(2,1)S(1)} %get-tuple-element.15, bf16[512,8320]{1,0:T(8,128)(2,1)} %bitcast.149), kind=kOutput, calls=%fused_computation.11 | convolution fusion | flops 403046400 | bytes 5079040 | tf_op jit(solution)/shard_map/expert_0/rh,rd->hd/dot_general | solution.py:84
  182.4 3.0 %fusion.1 = bf16[1,96,4096]{2,1,0:T(8,128)(2,1)S(1)} fusion(bf16[512,96]{0,1:T(8,128)(2,1)S(1)} %copy-done.11, bf16[512,8320]{1,0:T(8,128)(2,1)} %bitcast.140), kind=kOutput, calls=%fused_computation.10 | convolution fusion | flops 403046400 | bytes 5079040 | tf_op jit(solution)/shard_map/expert_1/rh,rd->hd/dot_general | solution.py:79
  185.4 3.1 %fusion.3 = bf16[1,96,4096]{2,1,0:T(8,128)(2,1)S(1)} fusion(bf16[512,96]{0,1:T(8,128)(2,1)S(1)} %copy-done.9, bf16[512,8320]{1,0:T(8,128)(2,1)} %bitcast.141), kind=kOutput, calls=%fused_computation.12 | convolution fusion | flops 403046400 | bytes 5079040 | tf_op jit(solution)/shard_map/expert_1/rh,rd->hd/dot_general | solution.py:84
  188.5 3.2 %fusion.4 = bf16[1,96,4096]{2,1,0:T(8,128)(2,1)S(1)} fusion(bf16[512,8320]{1,0:T(8,128)(2,1)} %bitcast.150, f32[512]{0:T(512)S(1)} %convert_reduce_fusion.1, f32[512,96]{0,1:T(8,128)S(1)} %copy-done.16, f32[512,96]{0,1:T(8,128)S(1)} %copy-done.17), kind=kOutput, calls=%fused_computation.13 | convolution fusion | flops 403390464 | bytes 5376000 | tf_op jit(solution)/shard_map/expert_0/rh,rd->hd/dot_general | solution.py:89
  191.8 1.9 pad_maximum_fusion.5
  193.7 51.7 %reduce-scatter.2.cloned.1.call-done = bf16[1,64,4224]{2,1,0:T(8,128)(2,1)} async-done(((bf16[16,64,4224]{2,1,0:T(8,128)(2,1)}), bf16[1,64,4224]{2,1,0:T(8,128)(2,1)}) %reduce-scatter.2.cloned.1.call-update) | async-done | bytes 540688 | tf_op jit(solution)/shard_map/reduce_scatter | solution.py:93
  245.4 1.2 reshape.187
  246.6 0.6 constant_dynamic-update-slice_fusion.15
  247.3 0.6 constant_dynamic-update-slice_fusion.14
  247.9 0.6 constant_dynamic-update-slice_fusion.13
  248.5 0.6 constant_dynamic-update-slice_fusion.12
  249.2 0.6 constant_dynamic-update-slice_fusion.11
  249.8 0.6 constant_dynamic-update-slice_fusion.10
  250.4 0.6 constant_dynamic-update-slice_fusion.9
  251.1 0.6 constant_dynamic-update-slice_fusion.8
  251.7 0.6 constant_dynamic-update-slice_fusion.7
  252.3 0.6 constant_dynamic-update-slice_fusion.6
  253.0 0.6 constant_dynamic-update-slice_fusion.5
  253.6 0.6 constant_dynamic-update-slice_fusion.4
  254.2 0.6 constant_dynamic-update-slice_fusion.3
  254.9 0.6 constant_dynamic-update-slice_fusion.2
  255.5 0.6 constant_dynamic-update-slice_fusion.1
  256.1 0.6 constant_dynamic-update-slice_fusion
  256.8 7.3 %all-to-all-start.2 = ((bf16[16,2,1,2,4224]{4,3,1,2,0:T(2,128)(2,1)}), bf16[16,2,1,2,4224]{4,3,1,2,0:T(2,128)(2,1)S(1)}, u32[]{:S(2)}, u32[]{:S(2)}) async-start(bf16[16,2,1,2,4224]{4,3,1,2,0:T(2,128)(2,1)} %constant_dynamic-update-slice_fusion), calls=%async_computation.3 | async-start | bytes 1081344 | tf_op jit(solution)/shard_map/all_to_all | solution.py:96
  264.0 3.0 %fusion.5 = bf16[1,96,4096]{2,1,0:T(8,128)(2,1)S(1)} fusion(bf16[512,8320]{1,0:T(8,128)(2,1)} %bitcast.142, f32[512]{0:T(512)S(1)} %convert_reduce_fusion, f32[512,96]{0,1:T(8,128)S(1)} %copy-done.13, f32[512,96]{0,1:T(8,128)S(1)} %copy-done.14), kind=kOutput, calls=%fused_computation.14 | convolution fusion | flops 403390464 | bytes 5376000 | tf_op jit(solution)/shard_map/expert_1/rh,rd->hd/dot_general | solution.py:89
  267.0 1.3 pad_maximum_fusion.7
  268.3 4.5 %all-to-all-done.2 = bf16[16,2,1,2,4224]{4,3,1,2,0:T(2,128)(2,1)S(1)} async-done(((bf16[16,2,1,2,4224]{4,3,1,2,0:T(2,128)(2,1)}), bf16[16,2,1,2,4224]{4,3,1,2,0:T(2,128)(2,1)S(1)}, u32[]{:S(2)}, u32[]{:S(2)}) %all-to-all-start.2) | async-done | bytes 540704 | tf_op jit(solution)/shard_map/all_to_all | solution.py:96
  272.8 0.4 copy.69
  273.2 0.2 reshape_reshape.3
  273.4 0.8 convolution_convert_fusion.10
  274.3 0.2 add_reduce_fusion
  274.5 0.8 fusion.61
  (60 shorter events, 1.3 us)
Async XLA Ops:
  7.2 2.6 copy-start
  7.2 80.8 %all-gather.3.cloned.1.call-start = ((), (), s32[]{:S(2)}) async-start(), calls=%async_computation.4 | async-start | bytes 9052160 | tf_op jit(solution)/shard_map/expert_0/all_gather | solution.py:53
  31.1 114.3 %all-gather.5.cloned.1.call-start = ((), (), s32[]{:S(2)}) async-start(), calls=%async_computation.5 | async-start | bytes 9052160 | tf_op jit(solution)/shard_map/expert_1/all_gather | solution.py:53
  31.2 16.9 %copy-start.1 = (bf16[2,96,4096]{2,1,0:T(8,128)(2,1)S(1)}, bf16[2,96,4096]{2,1,0:T(8,128)(2,1)}, u32[]{:S(2)}) copy-start(bf16[2,96,4096]{2,1,0:T(8,128)(2,1)} %param.12) | copy-start | bytes 4718596
  46.4 199.0 %reduce-scatter.2.cloned.1.call-start = ((), (), s32[]{:S(2)}) async-start(), calls=%async_computation.6 | async-start | bytes 9191424 | tf_op jit(solution)/shard_map/reduce_scatter | solution.py:93
  145.4 9.4 %copy-start.3 = (bf16[16,32,8320]{2,1,0:T(8,128)(2,1)S(1)}, bf16[16,32,8320]{2,1,0:T(8,128)(2,1)}, u32[]{:S(2)}) copy-start(bf16[16,32,8320]{2,1,0:T(8,128)(2,1)} %all-gather.5.cloned.1.call-done) | copy-start | bytes 25559044
  145.4 9.5 %copy-start.5 = (bf16[2,96,4096]{2,1,0:T(8,128)(2,1)S(1)}, bf16[2,96,4096]{2,1,0:T(8,128)(2,1)}, u32[]{:S(2)}) copy-start(bf16[2,96,4096]{2,1,0:T(8,128)(2,1)} %param.13) | copy-start | bytes 4718596
  149.4 9.2 %copy-start.12 = (f32[512,96]{0,1:T(8,128)}, f32[512,96]{0,1:T(8,128)S(1)}, u32[]{:S(2)}) copy-start(f32[512,96]{0,1:T(8,128)S(1)} %fusion.20) | copy-start | bytes 589828
  150.8 5.4 %copy-start.4 = (bf16[16,32,8320]{2,1,0:T(8,128)(2,1)S(1)}, bf16[16,32,8320]{2,1,0:T(8,128)(2,1)}, u32[]{:S(2)}) copy-start(bf16[16,32,8320]{2,1,0:T(8,128)(2,1)} %all-gather.3.cloned.1.call-done) | copy-start | bytes 25559044
  154.8 1.6 copy-start.2
  154.9 1.6 copy-start.15
  158.6 2.1 copy-start.6
  160.7 6.9 %copy-start.8 = (bf16[512,96]{0,1:T(8,128)(2,1)}, bf16[512,96]{0,1:T(8,128)(2,1)S(1)}, u32[]{:S(2)}) copy-start(bf16[512,96]{0,1:T(8,128)(2,1)S(1)} %get-tuple-element.16) | copy-start | bytes 294916
  160.7 6.9 %copy-start.10 = (bf16[512,96]{0,1:T(8,128)(2,1)}, bf16[512,96]{0,1:T(8,128)(2,1)S(1)}, u32[]{:S(2)}) copy-start(bf16[512,96]{0,1:T(8,128)(2,1)S(1)} %get-tuple-element.13) | copy-start | bytes 294916
  175.4 0.9 copy-start.7
  179.3 3.1 %copy-start.11 = (bf16[512,96]{0,1:T(8,128)(2,1)S(1)}, bf16[512,96]{0,1:T(8,128)(2,1)}, u32[]{:S(2)}) copy-start(bf16[512,96]{0,1:T(8,128)(2,1)} %copy-done.10) | copy-start | bytes 294916
  182.3 3.0 %copy-start.9 = (bf16[512,96]{0,1:T(8,128)(2,1)S(1)}, bf16[512,96]{0,1:T(8,128)(2,1)}, u32[]{:S(2)}) copy-start(bf16[512,96]{0,1:T(8,128)(2,1)} %copy-done.8) | copy-start | bytes 294916
  185.4 3.1 %copy-start.16 = (f32[512,96]{0,1:T(8,128)S(1)}, f32[512,96]{0,1:T(8,128)}, u32[]{:S(2)}) copy-start(f32[512,96]{0,1:T(8,128)} %fusion.26) | copy-start | bytes 589828
  185.4 3.1 %copy-start.17 = (f32[512,96]{0,1:T(8,128)S(1)}, f32[512,96]{0,1:T(8,128)}, u32[]{:S(2)}) copy-start(f32[512,96]{0,1:T(8,128)} %get-tuple-element.18) | copy-start | bytes 589828
  191.7 72.3 %copy-start.13 = (f32[512,96]{0,1:T(8,128)S(1)}, f32[512,96]{0,1:T(8,128)}, u32[]{:S(2)}) copy-start(f32[512,96]{0,1:T(8,128)} %copy-done.12) | copy-start | bytes 589828
  191.7 72.3 %copy-start.14 = (f32[512,96]{0,1:T(8,128)S(1)}, f32[512,96]{0,1:T(8,128)}, u32[]{:S(2)}) copy-start(f32[512,96]{0,1:T(8,128)} %get-tuple-element.17) | copy-start | bytes 589828
  256.8 16.1 %all-to-all-start.2 = ((bf16[16,2,1,2,4224]{4,3,1,2,0:T(2,128)(2,1)}), bf16[16,2,1,2,4224]{4,3,1,2,0:T(2,128)(2,1)S(1)}, u32[]{:S(2)}, u32[]{:S(2)}) async-start(bf16[16,2,1,2,4224]{4,3,1,2,0:T(2,128)(2,1)} %constant_dynamic-update-slice_fusion), calls=%async_computation.3 | async-start | bytes 1081344 | tf_op jit(solution)/shard_map/all_to_all | solution.py:96
Sparse Core Ops, SparseCore 0:
  31.3 56.6 all-gather.2
  90.3 55.0 all-gather.4
  175.5 69.8 reduce-scatter.1
